TPU v7x, 512 devices: a whole 4x8x8 slice. The times are simulated.
512 devices in a mesh: space: 64 (over x, y_hi, z), chan: 8 (over y_lo, core).
Axes of the slice: x: 4, y: 8 (y_hi: 2, y_lo: 4; y = y_hi * 4 + y_lo), z: 8, core: 2. Of those that a mesh axis runs over, the one named last changes fastest.
Arguments:
- activation: float32 [64, 2, 512, 256], P('space', None, 'chan'), may hold values from -6 to 6
- weight: bfloat16 [3, 3, 3, 512, 512], P(None, None, None, 'chan'), may hold values from -0.0546875 to 0.0546875
- conv_bias: float32 [512], P('chan'), may hold values from -3 to 3
Outputs:
- output: float32 [64, 2, 512, 256], P('space', None, 'chan')
All inputs are finite; a program needn't handle non-finite values.
Results may differ from a plain program's by a relative error of at most 0.0026.
Values may be sent and summed in bfloat16 or wider, within the bound.
No kernel may reach another device: no remote copies, remote signals or barrier semaphores. Data moves between devices by JAX's collectives and lax.ppermute only.
A program may use at most 64 MiB of HBM per device.

v0:
```python
import jax
import jax.numpy as jnp
from jax import lax
from jax.sharding import PartitionSpec as P

CY = 8
negative_slope = 0.3


def cross(lower_source, upper_source, axis, steps):
    count = lax.axis_size(axis)
    width = lax.axis_size("chan")
    run_y = width // 2
    pairs = []
    for source in range(count):
        for lane in range(width):
            place, core = divmod(lane, 2)
            target = (source + (steps if core == 0 else -steps)) % count
            crosses = source // CY % 2 != target // CY % 2
            moved = (place + run_y // 2) % run_y * 2 + core if crosses else lane
            pairs.append((source * width + lane, target * width + moved))
    on_first = lax.axis_index("chan") % 2 == 0
    sent = jnp.where(on_first, lower_source, upper_source)
    return lax.ppermute(sent, (axis, "chan"), pairs)


def swap(got):
    width = lax.axis_size("chan")
    on_first = lax.axis_index("chan") % 2 == 0
    swapped = lax.ppermute(got, "chan", [(lane, lane ^ 1) for lane in range(width)])
    return (jnp.where(on_first, got, swapped), jnp.where(on_first, swapped, got))


def conv(field, taps, padding):
    return lax.conv_general_dilated(
        field[None],
        taps,
        window_strides=(1, 1, 1),
        padding=padding,
        dimension_numbers=("NCDHW", "DHWOI", "NDCHW"),
        preferred_element_type=jnp.float32,
    )[0]


def body(activation, weight, conv_bias):
    size_x = activation.shape[1]
    size_y = CY
    size_z = activation.shape[3] // size_y
    own_block = activation[0].astype(jnp.bfloat16).transpose(1, 0, 2)
    gathered = lax.all_gather(own_block, "chan", axis=0, tiled=True)
    gathered = gathered.reshape(-1, size_x, size_y, size_z)
    own_part = conv(gathered, weight, ((1, 1), (1, 1), (1, 1)))
    width_in = gathered.shape[0]
    got = [
        cross(gathered[:, -1:], gathered[:, :1], "space", CY),
        cross(gathered[:, :, -1:], gathered[:, :, :1], "space", 1),
    ]
    corners_from, own_part = lax.optimization_barrier(
        (gathered[:, :: size_x - 1, :: size_y - 1], own_part)
    )
    got += [
        cross(corners_from[:, 1:, 1:], corners_from[:, :1, :1], "space", CY + 1),
        cross(corners_from[:, 1:, :1], corners_from[:, :1, 1:], "space", CY - 1),
    ]
    parity = lax.axis_index("chan") % 2
    on_first = parity == 0
    width = lax.axis_size("chan")
    pairs_core = [(lane, lane ^ 1) for lane in range(width)]
    mine_face = conv(
        got[0], lax.dynamic_slice_in_dim(weight, 2 * parity, 1, axis=0), ((0, 0), (1, 1), (1, 1))
    )
    sizes = [piece[0].size for piece in got]
    early = jnp.concatenate([piece.reshape(width_in, -1) for piece in got[:2]], axis=1)
    early_other = lax.ppermute(early, "chan", pairs_core)
    face_other = early_other[:, : sizes[0]].reshape(got[0].shape)
    row_other = early_other[:, sizes[0] :].reshape(got[1].shape)
    other_face = conv(
        face_other,
        lax.dynamic_slice_in_dim(weight, 2 - 2 * parity, 1, axis=0),
        ((0, 0), (1, 1), (1, 1)),
    )
    corners_got, own_part, mine_face, other_face, row_other = lax.optimization_barrier(
        (got[2:], own_part, mine_face, other_face, row_other)
    )
    late = jnp.concatenate([piece.reshape(width_in, -1) for piece in corners_got], axis=1)
    late_other = lax.ppermute(late, "chan", pairs_core)
    corner_a_other = late_other[:, : sizes[2]].reshape(got[2].shape)
    corner_b_other = late_other[:, sizes[2] :].reshape(got[3].shape)
    lower_row = jnp.where(on_first, got[1], row_other)
    upper_row = jnp.where(on_first, row_other, got[1])
    corner_ll = jnp.where(on_first, corners_got[0], corner_a_other)
    corner_hh = jnp.where(on_first, corner_a_other, corners_got[0])
    corner_lh = jnp.where(on_first, corners_got[1], corner_b_other)
    corner_hl = jnp.where(on_first, corner_b_other, corners_got[1])
    face_part = jnp.where(
        on_first,
        jnp.concatenate([mine_face, other_face], axis=0),
        jnp.concatenate([other_face, mine_face], axis=0),
    )
    place_y = (lax.axis_index("space") + 4) % 8
    lower_rim = jnp.concatenate([corner_ll, lower_row, corner_hl], axis=1)
    upper_rim = jnp.concatenate([corner_lh, upper_row, corner_hh], axis=1)
    lower_rim = jnp.where(place_y > 0, lower_rim, jnp.zeros_like(lower_rim))
    upper_rim = jnp.where(place_y < 7, upper_rim, jnp.zeros_like(upper_rim))
    lower_part = conv(lower_rim, weight[:, :1], ((0, 0), (0, 0), (1, 1)))
    upper_part = conv(upper_rim, weight[:, 2:], ((0, 0), (0, 0), (1, 1)))
    width_out = own_part.shape[1]
    middle = jnp.zeros((size_x, width_out, size_y - 2, size_z), jnp.float32)
    rim_part = jnp.concatenate([lower_part, middle, upper_part], axis=2)
    before = own_part + face_part + rim_part + conv_bias[None, :, None, None]
    result = jnp.maximum(before, negative_slope * before)
    return result.reshape(1, size_x, width_out, size_y * size_z)


def solution(mesh):
    placed = (P("space", None, "chan", None), P(None, None, None, "chan", None), P("chan"))
    return jax.shard_map(
        body, mesh=mesh, in_specs=placed, out_specs=P("space", None, "chan", None), check_vma=False
    )
```

profile of v0, /device:TPU:1, one launch (start us, length us, event | category | flops | bytes accessed | tf_op | source)
XLA Modules:
  0.0 60.7 jit_solution(9849114820241428272)
XLA Ops:
  0.0 0.9 %convert_element_type.8 = bf16[1,2,64,256]{3,2,1,0:T(8,128)(2,1)S(1)} convert(f32[1,2,64,256]{3,2,1,0:T(8,128)} %param.3) | non-fusion elementwise | flops 32768 | bytes 196608 | tf_op jit(solution)/shard_map/convert_element_type | solution.py:49
  1.0 21.7 %all_gather.3 = bf16[512,2,256]{2,1,0:T(2,128)(2,1)S(1)} all-gather(bf16[64,2,256]{2,1,0:T(2,128)(2,1)S(1)} %bitcast.122), channel_id=1, replica_groups=mesh['space'=64,'chan'=8] {'chan'}, dimensions={0}, use_global_device_ids=true | all-gather | bytes 589824 | tf_op jit(solution)/shard_map/all_gather | solution.py:50
  22.7 0.7 %copy.46 = bf16[512,2,256]{0,2,1:T(8,128)(2,1)S(1)} copy(bf16[512,2,256]{2,1,0:T(2,128)(2,1)S(1)} %all_gather.3) | data formatting | bytes 1048576 | tf_op jit(solution)/shard_map/all_gather | solution.py:50
  23.5 10.9 %collective-permute-start.3 = (bf16[512,2,1,32]{0,3,2,1:T(8,128)(2,1)S(1)}, bf16[512,2,1,32]{0,3,2,1:T(8,128)(2,1)S(1)}, u32[]{:S(2)}, u32[]{:S(2)}) collective-permute-start(bf16[512,2,1,32]{0,3,2,1:T(8,128)(2,1)S(1)} %slice_select_fusion.1), channel_id=1, source_target_pairs={{0,8},{1,509},{2,10},{3,511},{4,12},{5,505},{6,14},{7,507},{8,16},... | collective-permute-start | bytes 196616 | tf_op jit(solution)/shard_map/ppermute | solution.py:24
  34.4 1.9 %collective-permute-start.2 = (bf16[512,1,8,32]{0,3,2,1:T(8,128)(2,1)S(1)}, bf16[512,1,8,32]{0,3,2,1:T(8,128)(2,1)S(1)}, u32[]{:S(2)}, u32[]{:S(2)}) collective-permute-start(bf16[512,1,8,32]{0,3,2,1:T(8,128)(2,1)S(1)} %slice_select_fusion), channel_id=1, source_target_pairs={{0,68},{1,453},{2,70},{3,455},{4,64},{5,449},{6,66},{7,451},{8,76}... | collective-permute-start | bytes 786440 | tf_op jit(solution)/shard_map/ppermute | solution.py:24
  36.3 0.3 copy.82
  36.7 0.2 copy.50
  37.0 1.1 %copy-done.1 = bf16[3,3,3,64,512]{4,3,2,1,0:T(8,128)(2,1)S(1)} copy-done((bf16[3,3,3,64,512]{4,3,2,1,0:T(8,128)(2,1)S(1)}, bf16[3,3,3,64,512]{4,3,2,1,0:T(8,128)(2,1)}, u32[]{:S(2)}) %copy-start.1) | copy-done | bytes 1769496
  38.1 4.7 %convolution_select_fusion = f32[2,8,8,5,64]{4,2,3,1,0:T(8,128)S(1)} fusion(bf16[3,3,3,64,512]{4,3,2,1,0:T(8,128)(2,1)S(1)} %copy-done.1, bf16[512,2,8,1,7,2]{0,4,5,2,1,3:T(8,128)(2,1)S(1)} %slice.70, bf16[512,2,8,1,8,5]{0,4,5,2,1,3:T(8,128)(2,1)S(1)} %copy.50, pred[8,5]{0,1:T(8,128)(4,1)S(1)} %copy-done.2), kind=kOutput, calls=%fused_computation.2 | convolution fusion | flops 694853632 | bytes 2818088 | tf_op jit(solution)/shard_map/conv_general_dilated | solution.py:35
  43.0 1.9 %collective-permute-start.1 = (bf16[512,1,1,32]{0,3,2,1:T(8,128)(2,1)S(1)}, bf16[512,1,1,32]{0,3,2,1:T(8,128)(2,1)S(1)}, u32[]{:S(2)}, u32[]{:S(2)}) collective-permute-start(bf16[512,1,1,32]{0,3,2,1:T(8,128)(2,1)S(1)} %get-tuple-element.23), channel_id=1, source_target_pairs={{0,56},{1,461},{2,58},{3,463},{4,60},{5,457},{6,62},{7,459},{8,68}... | collective-permute-start | bytes 98312 | tf_op jit(solution)/shard_map/ppermute | solution.py:24
  44.9 4.8 %collective-permute-start = (bf16[512,1,1,32]{0,3,2,1:T(8,128)(2,1)S(1)}, bf16[512,1,1,32]{0,3,2,1:T(8,128)(2,1)S(1)}, u32[]{:S(2)}, u32[]{:S(2)}) collective-permute-start(bf16[512,1,1,32]{0,3,2,1:T(8,128)(2,1)S(1)} %get-tuple-element.24), channel_id=1, source_target_pairs={{0,76},{1,441},{2,78},{3,443},{4,72},{5,445},{6,74},{7,447},{8,84}... | collective-permute-start | bytes 98312 | tf_op jit(solution)/shard_map/ppermute | solution.py:24
  49.9 0.1 copy.83
  50.2 1.9 %collective-permute-start.4 = (bf16[512,320]{0,1:T(8,128)(2,1)S(1)}, bf16[512,320]{0,1:T(8,128)(2,1)S(1)}, u32[]{:S(2)}, u32[]{:S(2)}) collective-permute-start(bf16[512,320]{0,1:T(8,128)(2,1)S(1)} %pad_maximum_fusion), channel_id=1, source_target_pairs={{0,1},{1,0},{2,3},{3,2},{4,5},{5,4},{6,7},{7,6},{8,9},{9,8},{10,11... | collective-permute-start | bytes 983048 | tf_op jit(solution)/shard_map/ppermute | solution.py:74
  52.2 0.9 %convolution_select_fusion.2 = f32[1,8,8,5,64]{4,2,3,1,0:T(8,128)S(1)} fusion(bf16[3,3,3,64,512]{4,3,2,1,0:T(8,128)(2,1)S(1)} %copy-done.1, s32[]{:T(128)S(6)} %select_n.123, bf16[512,1,8,1,7,2]{0,4,5,2,3,1:T(8,128)(2,1)S(1)} %slice.74, bf16[512,1,8,1,8,5]{0,4,5,2,3,1:T(8,128)(2,1)S(1)} %copy.54, pred[8,5]{0,1:T(8,128)(4,1)S(1)} %copy-done.2), kind=kOutput, calls=%fused_computation.4 | convolution fusion | flops 174411776 | bytes 1131524 | tf_op jit(solution)/shard_map/conv_general_dilated | solution.py:35
  53.1 0.6 %collective-permute-done.4 = bf16[512,320]{0,1:T(8,128)(2,1)S(1)} collective-permute-done((bf16[512,320]{0,1:T(8,128)(2,1)S(1)}, bf16[512,320]{0,1:T(8,128)(2,1)S(1)}, u32[]{:S(2)}, u32[]{:S(2)}) %collective-permute-start.4) | collective-permute-done | bytes 327712 | tf_op jit(solution)/shard_map/ppermute | solution.py:74
  53.8 0.2 copy.84
  54.1 0.9 %convolution_select_fusion.1 = f32[1,8,8,5,64]{4,2,3,1,0:T(8,128)S(1)} fusion(bf16[3,3,3,64,512]{4,3,2,1,0:T(8,128)(2,1)S(1)} %copy-done.1, s32[]{:T(128)S(6)} %select_n.126, bf16[512,1,8,1,7,2]{0,4,5,2,3,1:T(8,128)(2,1)S(1)} %slice.79, bf16[512,1,8,1,8,5]{0,4,5,2,3,1:T(8,128)(2,1)S(1)} %copy.59, pred[8,5]{0,1:T(8,128)(4,1)S(1)} %copy-done.2), kind=kOutput, calls=%fused_computation.3 | convolution fusion | flops 174411776 | bytes 1131524 | tf_op jit(solution)/shard_map/conv_general_dilated | solution.py:35
  55.2 2.1 %collective-permute-start.5 = (bf16[512,64]{0,1:T(8,128)(2,1)S(1)}, bf16[512,64]{0,1:T(8,128)(2,1)S(1)}, u32[]{:S(2)}, u32[]{:S(2)}) collective-permute-start(bf16[512,64]{0,1:T(8,128)(2,1)S(1)} %pad_maximum_fusion.1), channel_id=1, source_target_pairs={{0,1},{1,0},{2,3},{3,2},{4,5},{5,4},{6,7},{7,6},{8,9},{9,8},{10,11... | collective-permute-start | bytes 196616 | tf_op jit(solution)/shard_map/ppermute | solution.py:86
  57.2 1.1 %collective-permute-done.5 = bf16[512,64]{0,1:T(8,128)(2,1)S(1)} collective-permute-done((bf16[512,64]{0,1:T(8,128)(2,1)S(1)}, bf16[512,64]{0,1:T(8,128)(2,1)S(1)}, u32[]{:S(2)}, u32[]{:S(2)}) %collective-permute-start.5) | collective-permute-done | bytes 65568 | tf_op jit(solution)/shard_map/ppermute | solution.py:86
  58.4 0.1 copy.85
  58.6 0.3 convolution_select_fusion.4
  59.3 0.3 convolution_select_fusion.3
  59.7 0.2 multiply_maximum_fusion
  59.9 0.8 %copy.79 = f32[1,2,64,256]{3,2,1,0:T(8,128)} copy(f32[1,2,64,256]{2,3,1,0:T(8,128)S(1)} %bitcast.116) | data formatting | bytes 262144 | tf_op jit(solution)/shard_map/reshape | solution.py:112
  (51 shorter events, 1.4 us)
Async XLA Ops:
  23.5 26.7 %collective-permute-start.3 = (bf16[512,2,1,32]{0,3,2,1:T(8,128)(2,1)S(1)}, bf16[512,2,1,32]{0,3,2,1:T(8,128)(2,1)S(1)}, u32[]{:S(2)}, u32[]{:S(2)}) collective-permute-start(bf16[512,2,1,32]{0,3,2,1:T(8,128)(2,1)S(1)} %slice_select_fusion.1), channel_id=1, source_target_pairs={{0,8},{1,509},{2,10},{3,511},{4,12},{5,505},{6,14},{7,507},{8,16},... | collective-permute-start | bytes 196616 | tf_op jit(solution)/shard_map/ppermute | solution.py:24
  34.4 15.4 %collective-permute-start.2 = (bf16[512,1,8,32]{0,3,2,1:T(8,128)(2,1)S(1)}, bf16[512,1,8,32]{0,3,2,1:T(8,128)(2,1)S(1)}, u32[]{:S(2)}, u32[]{:S(2)}) collective-permute-start(bf16[512,1,8,32]{0,3,2,1:T(8,128)(2,1)S(1)} %slice_select_fusion), channel_id=1, source_target_pairs={{0,68},{1,453},{2,70},{3,455},{4,64},{5,449},{6,66},{7,451},{8,76}... | collective-permute-start | bytes 786440 | tf_op jit(solution)/shard_map/ppermute | solution.py:24
  36.6 1.5 %copy-start.1 = (bf16[3,3,3,64,512]{4,3,2,1,0:T(8,128)(2,1)S(1)}, bf16[3,3,3,64,512]{4,3,2,1,0:T(8,128)(2,1)}, u32[]{:S(2)}) copy-start(bf16[3,3,3,64,512]{4,3,2,1,0:T(8,128)(2,1)} %param.4) | copy-start | bytes 5308420
  36.7 1.5 %copy-start.2 = (pred[8,5]{0,1:T(8,128)(4,1)S(1)}, pred[8,5]{0,1:T(8,128)(4,1)}, u32[]{:S(2)}) copy-start(pred[8,5]{0,1:T(8,128)(4,1)} %constant.75) | copy-start | bytes 124
  43.0 12.2 %collective-permute-start.1 = (bf16[512,1,1,32]{0,3,2,1:T(8,128)(2,1)S(1)}, bf16[512,1,1,32]{0,3,2,1:T(8,128)(2,1)S(1)}, u32[]{:S(2)}, u32[]{:S(2)}) collective-permute-start(bf16[512,1,1,32]{0,3,2,1:T(8,128)(2,1)S(1)} %get-tuple-element.23), channel_id=1, source_target_pairs={{0,56},{1,461},{2,58},{3,463},{4,60},{5,457},{6,62},{7,459},{8,68}... | collective-permute-start | bytes 98312 | tf_op jit(solution)/shard_map/ppermute | solution.py:24
  44.9 10.2 %collective-permute-start = (bf16[512,1,1,32]{0,3,2,1:T(8,128)(2,1)S(1)}, bf16[512,1,1,32]{0,3,2,1:T(8,128)(2,1)S(1)}, u32[]{:S(2)}, u32[]{:S(2)}) collective-permute-start(bf16[512,1,1,32]{0,3,2,1:T(8,128)(2,1)S(1)} %get-tuple-element.24), channel_id=1, source_target_pairs={{0,76},{1,441},{2,78},{3,443},{4,72},{5,445},{6,74},{7,447},{8,84}... | collective-permute-start | bytes 98312 | tf_op jit(solution)/shard_map/ppermute | solution.py:24
  50.2 3.5 %collective-permute-start.4 = (bf16[512,320]{0,1:T(8,128)(2,1)S(1)}, bf16[512,320]{0,1:T(8,128)(2,1)S(1)}, u32[]{:S(2)}, u32[]{:S(2)}) collective-permute-start(bf16[512,320]{0,1:T(8,128)(2,1)S(1)} %pad_maximum_fusion), channel_id=1, source_target_pairs={{0,1},{1,0},{2,3},{3,2},{4,5},{5,4},{6,7},{7,6},{8,9},{9,8},{10,11... | collective-permute-start | bytes 983048 | tf_op jit(solution)/shard_map/ppermute | solution.py:74
  55.2 3.1 %collective-permute-start.5 = (bf16[512,64]{0,1:T(8,128)(2,1)S(1)}, bf16[512,64]{0,1:T(8,128)(2,1)S(1)}, u32[]{:S(2)}, u32[]{:S(2)}) collective-permute-start(bf16[512,64]{0,1:T(8,128)(2,1)S(1)} %pad_maximum_fusion.1), channel_id=1, source_target_pairs={{0,1},{1,0},{2,3},{3,2},{4,5},{5,4},{6,7},{7,6},{8,9},{9,8},{10,11... | collective-permute-start | bytes 196616 | tf_op jit(solution)/shard_map/ppermute | solution.py:86
  59.0 0.7 %copy-start = (f32[64]{0:T(128)S(1)}, f32[64]{0:T(128)}, u32[]{:S(2)}) copy-start(f32[64]{0:T(128)} %param.5) | copy-start | bytes 772
where the time goes:
time: 61 us; the launch traced here: 60.7 us
  starting transfers between devices  23.5 us (39%)
  blocking collectives  21.7 us (36%)
  matrix products  7.21 us (12%)
  local copies, waits for them, and re-layouts  4.76 us (8%)
  waiting for transfers between devices  1.69 us (3%)
  other arithmetic  1.23 us (2%)
    all_gather x1, blocking collectives, body(): gathered = lax.all_gather(own_block, 'chan', axis=0, tiled=True)  21.7 us
    ppermute x4, starting transfers between devices, cross(): return lax.ppermute(sent, (axis, 'chan'), pairs)  19.6 us
    conv_general_dilated x5, matrix products, conv(): lax.conv_general_dilated(field[None], taps, window_strides=(1, 1, 1), pad...  7.21 us
    ppermute x1, starting transfers between devices, body(): late_other = lax.ppermute(late, 'chan', pairs_core)  2.06 us
    unnamed x14, local copies, waits for them, and re-layouts  2.03 us
    ppermute x1, starting transfers between devices, body(): early_other = lax.ppermute(early, 'chan', pairs_core)  1.92 us
  transfers between devices with their start and end apart: 6, of which 2 were waited for; matrix products, arithmetic and copies ran while one was open for 13% of the time, Pallas kernels for 0%

commit v1 on v0

--- a/solution.py
+++ b/solution.py
@@ -47,7 +47,9 @@
     size_y = CY
     size_z = activation.shape[3] // size_y
     own_block = activation[0].astype(jnp.bfloat16).transpose(1, 0, 2)
-    gathered = lax.all_gather(own_block, "chan", axis=0, tiled=True)
+    gathered = jnp.concatenate(
+        lax.all_to_all(jnp.stack([own_block] * lax.axis_size("chan")), "chan", 0, 0), axis=0
+    )
     gathered = gathered.reshape(-1, size_x, size_y, size_z)
     own_part = conv(gathered, weight, ((1, 1), (1, 1), (1, 1)))
     width_in = gathered.shape[0]

time: 61 us -> 67.4 us (1.10)
  the two profiles are of different devices: /device:TPU:1 before, /device:TPU:9 now
where the time goes in v1:
time: 67.4 us; the launch traced here: 67 us
  starting transfers between devices  36 us (53%)
  waiting for transfers between devices  16.6 us (25%)
  matrix products  7.26 us (11%)
  local copies, waits for them, and re-layouts  5.46 us (8%)
  other arithmetic  1.22 us (2%)
    ppermute x4, starting transfers between devices, cross(): return lax.ppermute(sent, (axis, 'chan'), pairs)  22.5 us
    all_to_all x1, waiting for transfers between devices, body(): lax.all_to_all(jnp.stack([own_block] * lax.axis_size('chan')), 'chan', 0, 0)  11.7 us
    all_to_all x1, starting transfers between devices, body(): lax.all_to_all(jnp.stack([own_block] * lax.axis_size('chan')), 'chan', 0, 0)  9.54 us
    conv_general_dilated x5, matrix products, conv(): lax.conv_general_dilated(field[None], taps, window_strides=(1, 1, 1), pad...  7.26 us
    ppermute x4, waiting for transfers between devices, cross(): return lax.ppermute(sent, (axis, 'chan'), pairs)  3.23 us
    ppermute x1, starting transfers between devices, body(): late_other = lax.ppermute(late, 'chan', pairs_core)  2.04 us
    ppermute x1, starting transfers between devices, body(): early_other = lax.ppermute(early, 'chan', pairs_core)  1.92 us
  transfers between devices with their start and end apart: 7, of which 4 were waited for; matrix products, arithmetic and copies ran while one was open for 12% of the time, Pallas kernels for 0%

profile of v1, /device:TPU:9, one launch (start us, length us, event | category | flops | bytes accessed | tf_op | source)
XLA Modules:
  0.0 67.0 jit_solution(18172971912420338242)
XLA Ops:
  0.0 0.9 %convert_bitcast_fusion = bf16[64,2,256]{2,0,1:T(8,128)(2,1)S(1)} fusion(f32[1,2,64,256]{3,2,1,0:T(8,128)} %param.3), kind=kLoop, calls=%fused_computation.67 | loop fusion | flops 32768 | bytes 196608 | tf_op jit(solution)/shard_map/transpose | solution.py:49
  0.9 0.8 %stack.2 = bf16[8,64,2,256]{3,1,2,0:T(8,128)(2,1)} broadcast(bf16[64,2,256]{2,0,1:T(8,128)(2,1)S(1)} %convert_bitcast_fusion), dimensions={1,2,3} | broadcast | bytes 589824 | tf_op jit(solution)/shard_map/stack | solution.py:51
  1.8 9.5 %all-to-all-start = ((bf16[8,64,2,256]{3,1,2,0:T(8,128)(2,1)}), bf16[8,64,2,256]{3,1,2,0:T(8,128)(2,1)S(1)}, u32[]{:S(2)}, u32[]{:S(2)}) async-start(bf16[8,64,2,256]{3,1,2,0:T(8,128)(2,1)} %stack.2), calls=%async_computation | async-start | bytes 1048576 | tf_op jit(solution)/shard_map/all_to_all | solution.py:51
  11.4 11.7 %all-to-all-done = bf16[8,64,2,256]{3,1,2,0:T(8,128)(2,1)S(1)} async-done(((bf16[8,64,2,256]{3,1,2,0:T(8,128)(2,1)}), bf16[8,64,2,256]{3,1,2,0:T(8,128)(2,1)S(1)}, u32[]{:S(2)}, u32[]{:S(2)}) %all-to-all-start) | async-done | bytes 524320 | tf_op jit(solution)/shard_map/all_to_all | solution.py:51
  23.1 0.6 copy.52
  23.7 0.6 reshape_reshape.3
  24.3 0.6 reshape.181
  25.0 0.3 copy.89
  25.3 13.8 %collective-permute-start.3 = (bf16[512,2,1,32]{0,3,2,1:T(8,128)(2,1)S(1)}, bf16[512,2,1,32]{0,3,2,1:T(8,128)(2,1)S(1)}, u32[]{:S(2)}, u32[]{:S(2)}) collective-permute-start(bf16[512,2,1,32]{0,3,2,1:T(8,128)(2,1)S(1)} %bitcast_select_fusion.1), channel_id=1, source_target_pairs={{0,8},{1,509},{2,10},{3,511},{4,12},{5,505},{6,14},{7,507},{8,16},... | collective-permute-start | bytes 196616 | tf_op jit(solution)/shard_map/ppermute | solution.py:24
  39.2 0.2 copy.56
  39.4 4.7 %convolution_select_fusion = f32[2,8,8,5,64]{4,2,3,1,0:T(8,128)S(1)} fusion(bf16[3,3,3,64,512]{4,3,2,1,0:T(8,128)(2,1)S(1)} %copy-done.1, bf16[512,2,8,1,7,2]{0,4,5,2,1,3:T(8,128)(2,1)S(1)} %slice.70, bf16[512,2,8,1,8,5]{0,4,5,2,1,3:T(8,128)(2,1)S(1)} %copy.56, pred[8,5]{0,1:T(8,128)(4,1)S(1)} %copy-done.2), kind=kOutput, calls=%fused_computation.2 | convolution fusion | flops 694853632 | bytes 2818088 | tf_op jit(solution)/shard_map/conv_general_dilated | solution.py:35
  44.2 1.9 %collective-permute-start.2 = (bf16[512,1,8,32]{0,3,2,1:T(8,128)(2,1)S(1)}, bf16[512,1,8,32]{0,3,2,1:T(8,128)(2,1)S(1)}, u32[]{:S(2)}, u32[]{:S(2)}) collective-permute-start(bf16[512,1,8,32]{0,3,2,1:T(8,128)(2,1)S(1)} %slice_select_fusion), channel_id=1, source_target_pairs={{0,68},{1,453},{2,70},{3,455},{4,64},{5,449},{6,66},{7,451},{8,76}... | collective-permute-start | bytes 786440 | tf_op jit(solution)/shard_map/ppermute | solution.py:24
  46.2 1.9 %collective-permute-start.1 = (bf16[512,1,1,32]{0,3,2,1:T(8,128)(2,1)S(1)}, bf16[512,1,1,32]{0,3,2,1:T(8,128)(2,1)S(1)}, u32[]{:S(2)}, u32[]{:S(2)}) collective-permute-start(bf16[512,1,1,32]{0,3,2,1:T(8,128)(2,1)S(1)} %get-tuple-element.21), channel_id=1, source_target_pairs={{0,56},{1,461},{2,58},{3,463},{4,60},{5,457},{6,62},{7,459},{8,68}... | collective-permute-start | bytes 98312 | tf_op jit(solution)/shard_map/ppermute | solution.py:24
  48.1 4.8 %collective-permute-start = (bf16[512,1,1,32]{0,3,2,1:T(8,128)(2,1)S(1)}, bf16[512,1,1,32]{0,3,2,1:T(8,128)(2,1)S(1)}, u32[]{:S(2)}, u32[]{:S(2)}) collective-permute-start(bf16[512,1,1,32]{0,3,2,1:T(8,128)(2,1)S(1)} %get-tuple-element.22), channel_id=1, source_target_pairs={{0,76},{1,441},{2,78},{3,443},{4,72},{5,445},{6,74},{7,447},{8,84}... | collective-permute-start | bytes 98312 | tf_op jit(solution)/shard_map/ppermute | solution.py:24
  53.0 3.2 %collective-permute-done.2 = bf16[512,1,8,32]{0,3,2,1:T(8,128)(2,1)S(1)} collective-permute-done((bf16[512,1,8,32]{0,3,2,1:T(8,128)(2,1)S(1)}, bf16[512,1,8,32]{0,3,2,1:T(8,128)(2,1)S(1)}, u32[]{:S(2)}, u32[]{:S(2)}) %collective-permute-start.2) | collective-permute-done | bytes 262176 | tf_op jit(solution)/shard_map/ppermute | solution.py:24
  56.6 1.9 %collective-permute-start.4 = (bf16[512,320]{0,1:T(8,128)(2,1)S(1)}, bf16[512,320]{0,1:T(8,128)(2,1)S(1)}, u32[]{:S(2)}, u32[]{:S(2)}) collective-permute-start(bf16[512,320]{0,1:T(8,128)(2,1)S(1)} %pad_maximum_fusion), channel_id=1, source_target_pairs={{0,1},{1,0},{2,3},{3,2},{4,5},{5,4},{6,7},{7,6},{8,9},{9,8},{10,11... | collective-permute-start | bytes 983048 | tf_op jit(solution)/shard_map/ppermute | solution.py:76
  58.5 0.9 %convolution_select_fusion.2 = f32[1,8,8,5,64]{4,2,3,1,0:T(8,128)S(1)} fusion(bf16[3,3,3,64,512]{4,3,2,1,0:T(8,128)(2,1)S(1)} %copy-done.1, s32[]{:T(128)S(6)} %select_n.123, bf16[512,1,8,1,7,2]{0,4,5,2,3,1:T(8,128)(2,1)S(1)} %slice.74, bf16[512,1,8,1,8,5]{0,4,5,2,3,1:T(8,128)(2,1)S(1)} %copy.60, pred[8,5]{0,1:T(8,128)(4,1)S(1)} %copy-done.2), kind=kOutput, calls=%fused_computation.4 | convolution fusion | flops 174411776 | bytes 1131524 | tf_op jit(solution)/shard_map/conv_general_dilated | solution.py:35
  59.5 0.6 collective-permute-done.4
  60.5 0.9 %convolution_select_fusion.1 = f32[1,8,8,5,64]{4,2,3,1,0:T(8,128)S(1)} fusion(bf16[3,3,3,64,512]{4,3,2,1,0:T(8,128)(2,1)S(1)} %copy-done.1, s32[]{:T(128)S(6)} %select_n.126, bf16[512,1,8,1,7,2]{0,4,5,2,3,1:T(8,128)(2,1)S(1)} %slice.79, bf16[512,1,8,1,8,5]{0,4,5,2,3,1:T(8,128)(2,1)S(1)} %copy.66, pred[8,5]{0,1:T(8,128)(4,1)S(1)} %copy-done.2), kind=kOutput, calls=%fused_computation.3 | convolution fusion | flops 174411776 | bytes 1131524 | tf_op jit(solution)/shard_map/conv_general_dilated | solution.py:35
  61.5 2.0 %collective-permute-start.5 = (bf16[512,64]{0,1:T(8,128)(2,1)S(1)}, bf16[512,64]{0,1:T(8,128)(2,1)S(1)}, u32[]{:S(2)}, u32[]{:S(2)}) collective-permute-start(bf16[512,64]{0,1:T(8,128)(2,1)S(1)} %pad_maximum_fusion.1), channel_id=1, source_target_pairs={{0,1},{1,0},{2,3},{3,2},{4,5},{5,4},{6,7},{7,6},{8,9},{9,8},{10,11... | collective-permute-start | bytes 196616 | tf_op jit(solution)/shard_map/ppermute | solution.py:88
  63.6 1.1 %collective-permute-done.5 = bf16[512,64]{0,1:T(8,128)(2,1)S(1)} collective-permute-done((bf16[512,64]{0,1:T(8,128)(2,1)S(1)}, bf16[512,64]{0,1:T(8,128)(2,1)S(1)}, u32[]{:S(2)}, u32[]{:S(2)}) %collective-permute-start.5) | collective-permute-done | bytes 65568 | tf_op jit(solution)/shard_map/ppermute | solution.py:88
  65.0 0.3 convolution_select_fusion.4
  65.6 0.3 convolution_select_fusion.3
  66.3 0.8 %copy.86 = f32[1,2,64,256]{3,2,1,0:T(8,128)} copy(f32[1,2,64,256]{2,3,1,0:T(8,128)S(1)} %bitcast.119) | data formatting | bytes 262144 | tf_op jit(solution)/shard_map/reshape | solution.py:114
  (55 shorter events, 1.9 us)
Async XLA Ops:
  1.8 21.3 %all-to-all-start = ((bf16[8,64,2,256]{3,1,2,0:T(8,128)(2,1)}), bf16[8,64,2,256]{3,1,2,0:T(8,128)(2,1)S(1)}, u32[]{:S(2)}, u32[]{:S(2)}) async-start(bf16[8,64,2,256]{3,1,2,0:T(8,128)(2,1)} %stack.2), calls=%async_computation | async-start | bytes 1048576 | tf_op jit(solution)/shard_map/all_to_all | solution.py:51
  25.3 14.2 %copy-start.1 = (bf16[3,3,3,64,512]{4,3,2,1,0:T(8,128)(2,1)S(1)}, bf16[3,3,3,64,512]{4,3,2,1,0:T(8,128)(2,1)}, u32[]{:S(2)}) copy-start(bf16[3,3,3,64,512]{4,3,2,1,0:T(8,128)(2,1)} %param.4) | copy-start | bytes 5308420
  25.3 14.2 %copy-start.2 = (pred[8,5]{0,1:T(8,128)(4,1)S(1)}, pred[8,5]{0,1:T(8,128)(4,1)}, u32[]{:S(2)}) copy-start(pred[8,5]{0,1:T(8,128)(4,1)} %constant.75) | copy-start | bytes 124
  25.3 31.2 %collective-permute-start.3 = (bf16[512,2,1,32]{0,3,2,1:T(8,128)(2,1)S(1)}, bf16[512,2,1,32]{0,3,2,1:T(8,128)(2,1)S(1)}, u32[]{:S(2)}, u32[]{:S(2)}) collective-permute-start(bf16[512,2,1,32]{0,3,2,1:T(8,128)(2,1)S(1)} %bitcast_select_fusion.1), channel_id=1, source_target_pairs={{0,8},{1,509},{2,10},{3,511},{4,12},{5,505},{6,14},{7,507},{8,16},... | collective-permute-start | bytes 196616 | tf_op jit(solution)/shard_map/ppermute | solution.py:24
  44.2 12.0 %collective-permute-start.2 = (bf16[512,1,8,32]{0,3,2,1:T(8,128)(2,1)S(1)}, bf16[512,1,8,32]{0,3,2,1:T(8,128)(2,1)S(1)}, u32[]{:S(2)}, u32[]{:S(2)}) collective-permute-start(bf16[512,1,8,32]{0,3,2,1:T(8,128)(2,1)S(1)} %slice_select_fusion), channel_id=1, source_target_pairs={{0,68},{1,453},{2,70},{3,455},{4,64},{5,449},{6,66},{7,451},{8,76}... | collective-permute-start | bytes 786440 | tf_op jit(solution)/shard_map/ppermute | solution.py:24
  46.2 15.3 %collective-permute-start.1 = (bf16[512,1,1,32]{0,3,2,1:T(8,128)(2,1)S(1)}, bf16[512,1,1,32]{0,3,2,1:T(8,128)(2,1)S(1)}, u32[]{:S(2)}, u32[]{:S(2)}) collective-permute-start(bf16[512,1,1,32]{0,3,2,1:T(8,128)(2,1)S(1)} %get-tuple-element.21), channel_id=1, source_target_pairs={{0,56},{1,461},{2,58},{3,463},{4,60},{5,457},{6,62},{7,459},{8,68}... | collective-permute-start | bytes 98312 | tf_op jit(solution)/shard_map/ppermute | solution.py:24
  48.1 13.3 %collective-permute-start = (bf16[512,1,1,32]{0,3,2,1:T(8,128)(2,1)S(1)}, bf16[512,1,1,32]{0,3,2,1:T(8,128)(2,1)S(1)}, u32[]{:S(2)}, u32[]{:S(2)}) collective-permute-start(bf16[512,1,1,32]{0,3,2,1:T(8,128)(2,1)S(1)} %get-tuple-element.22), channel_id=1, source_target_pairs={{0,76},{1,441},{2,78},{3,443},{4,72},{5,445},{6,74},{7,447},{8,84}... | collective-permute-start | bytes 98312 | tf_op jit(solution)/shard_map/ppermute | solution.py:24
  56.6 3.5 %collective-permute-start.4 = (bf16[512,320]{0,1:T(8,128)(2,1)S(1)}, bf16[512,320]{0,1:T(8,128)(2,1)S(1)}, u32[]{:S(2)}, u32[]{:S(2)}) collective-permute-start(bf16[512,320]{0,1:T(8,128)(2,1)S(1)} %pad_maximum_fusion), channel_id=1, source_target_pairs={{0,1},{1,0},{2,3},{3,2},{4,5},{5,4},{6,7},{7,6},{8,9},{9,8},{10,11... | collective-permute-start | bytes 983048 | tf_op jit(solution)/shard_map/ppermute | solution.py:76
  61.5 3.1 %collective-permute-start.5 = (bf16[512,64]{0,1:T(8,128)(2,1)S(1)}, bf16[512,64]{0,1:T(8,128)(2,1)S(1)}, u32[]{:S(2)}, u32[]{:S(2)}) collective-permute-start(bf16[512,64]{0,1:T(8,128)(2,1)S(1)} %pad_maximum_fusion.1), channel_id=1, source_target_pairs={{0,1},{1,0},{2,3},{3,2},{4,5},{5,4},{6,7},{7,6},{8,9},{9,8},{10,11... | collective-permute-start | bytes 196616 | tf_op jit(solution)/shard_map/ppermute | solution.py:88
  65.3 0.7 %copy-start = (f32[64]{0:T(128)S(1)}, f32[64]{0:T(128)}, u32[]{:S(2)}) copy-start(f32[64]{0:T(128)} %param.5) | copy-start | bytes 772
